TPU v7x, 512 devices: a whole 4x8x8 slice. The times are simulated.
512 devices in a mesh: dp: 32 (over z, x), fsdp: 16 (over y, core).
Axes of the slice: x: 4, y: 8, z: 8, core: 2. Of those that a mesh axis runs over, the one named last changes fastest.
Arguments:
- projected: bfloat16 [65536, 2304], P(('dp', 'fsdp')), may hold values from -7.03125 to 7.03125
- out_weight: bfloat16 [768, 1536], P('fsdp'), may hold values from -0.21875 to 0.21875
- kernel: float32 [31, 1536], replicated, may hold values from -2 to 2
- cotangent: bfloat16 [65536, 1536], P(('dp', 'fsdp')), may hold values from -6 to 6
- send_rows: int32 [65536], P(('dp', 'fsdp')), may hold values from -1 to 127, as said below
- compute_src: int32 [65536], P(('dp', 'fsdp')), may hold values from -1 to 127, as said below
- segment: int32 [65536], P(('dp', 'fsdp')), may hold values from -1 to 3, as said below
Outputs:
- block_out: bfloat16 [65536, 1536], P(('dp', 'fsdp'))
- projected_grad: bfloat16 [65536, 2304], P(('dp', 'fsdp'))
- out_weight_grad: float32 [768, 1536], P('fsdp')
- kernel_grad: float32 [31, 1536], replicated
Inputs may be any that keep to these rules, and one draw needn't show every extreme that they name: `send_rows`: A device's 128 entries are 32 blocks of 4, block t for index t of dp at the same fsdp index; each lists rows of the device's own block of projected, each row at most once, filled entries first in a block and -1 after them. In every draw some device of each fsdp index fills all its entries. `compute_src`: on device (t, f), a row holds s * 4 + k when it receives entry t * 4 + k of device (s, f); every filled entry of send_rows is received by exactly one row, and a row holds -1 when it receives nothing. Filled rows come first. In every draw some device of each fsdp index receives a full block from every device. On each device, rows with compute_src = -1 hold -1, the others hold segment numbers from 0 that never fall along the rows.
All inputs are finite; a program needn't handle non-finite values.
Results may differ from a plain program's by a relative error of at most 0.018.
Values may be sent and summed in bfloat16 or wider, within the bound.
No kernel may reach another device: no remote copies, remote signals or barrier semaphores. Data moves between devices by JAX's collectives and lax.ppermute only.
A program may use at most 128 MiB of HBM per device.

v0:
```python
import jax
import jax.numpy as jnp
from jax import lax
from jax.sharding import PartitionSpec as P

HEADS = 8
HEAD_DIM = 96


def split_heads(frames):
    length = frames.shape[0]
    inner_width = HEADS * HEAD_DIM
    query_part = frames[:, :inner_width].reshape(length, HEADS, HEAD_DIM)
    key_part = frames[:, inner_width : 2 * inner_width].reshape(length, HEADS, HEAD_DIM)
    value_part = frames[:, 2 * inner_width :].reshape(length, HEADS, HEAD_DIM)
    return (query_part, key_part, value_part)


def attend(frames, segment):
    query_part, key_part, value_part = split_heads(frames)
    scores = jnp.einsum(
        "qhd,khd->hqk", query_part, key_part, preferred_element_type=jnp.float32
    ) * HEAD_DIM ** (-0.5)
    inside = segment[:, None] == segment[None, :]
    scores = jnp.where(inside[None], scores, -1e30)
    highest = jnp.max(scores, axis=2, keepdims=True)
    weights = jnp.exp(scores - highest)
    soft_probs = weights / jnp.sum(weights, axis=2, keepdims=True)
    rounded = soft_probs.astype(jnp.bfloat16)
    context = jnp.einsum("hqk,khd->qhd", rounded, value_part, preferred_element_type=jnp.float32)
    return (
        context.reshape(frames.shape[0], HEADS * HEAD_DIM).astype(jnp.bfloat16),
        soft_probs,
        rounded,
    )


def attend_back(frames, soft_probs, rounded, context_grad):
    query_part, key_part, value_part = split_heads(frames)
    length = frames.shape[0]
    inner_width = HEADS * HEAD_DIM
    upstream = context_grad.reshape(length, HEADS, HEAD_DIM)
    value_grad = jnp.einsum("hqk,qhd->khd", rounded, upstream, preferred_element_type=jnp.float32)
    prob_grad = jnp.einsum("qhd,khd->hqk", upstream, value_part, preferred_element_type=jnp.float32)
    score_grad = soft_probs * (prob_grad - jnp.sum(prob_grad * soft_probs, axis=2, keepdims=True))
    score_grad = (score_grad * HEAD_DIM ** (-0.5)).astype(jnp.bfloat16)
    query_grad = jnp.einsum(
        "hqk,khd->qhd", score_grad, key_part, preferred_element_type=jnp.float32
    )
    key_grad = jnp.einsum(
        "hqk,qhd->khd", score_grad, query_part, preferred_element_type=jnp.float32
    )
    return jnp.concatenate(
        [
            query_grad.reshape(length, inner_width).astype(jnp.bfloat16),
            key_grad.reshape(length, inner_width).astype(jnp.bfloat16),
            value_grad.reshape(length, inner_width).astype(jnp.bfloat16),
        ],
        axis=1,
    )


def finish(mixed, kernel, segment):
    length = mixed.shape[0]
    tap_count = kernel.shape[0]
    half_span = (tap_count - 1) // 2
    signal = mixed.astype(jnp.float32)
    padded = jnp.pad(signal, ((half_span, half_span), (0, 0)))
    neighbours = jnp.pad(segment, (half_span, half_span), constant_values=-2)
    convolved = jnp.zeros_like(signal)
    for offset in range(tap_count):
        matching = (neighbours[offset : offset + length] == segment).astype(jnp.float32)
        convolved = (
            convolved + kernel[offset] * padded[offset : offset + length] * matching[:, None]
        )
    return signal + jax.nn.silu(convolved)


def body(projected, out_weight, kernel, cotangent, send_rows, compute_src, segment):
    row_count = projected.shape[0]
    present = send_rows >= 0
    outgoing = jnp.take(projected, jnp.maximum(send_rows, 0), axis=0)
    outgoing = jnp.where(present[:, None], outgoing, jnp.zeros_like(outgoing))
    incoming = lax.all_to_all(outgoing, "dp", split_axis=0, concat_axis=0, tiled=True)
    filled = compute_src >= 0
    frames = jnp.take(incoming, jnp.maximum(compute_src, 0), axis=0)
    frames = jnp.where(filled[:, None], frames, jnp.zeros_like(frames))
    context, soft_probs, rounded = attend(frames, segment)
    columns = context
    mixed_sums = jnp.dot(
        columns,
        lax.all_gather(out_weight, "fsdp", axis=0, tiled=True),
        preferred_element_type=jnp.float32,
    )
    mixed = mixed_sums.astype(jnp.bfloat16)
    result, pullback = jax.vjp(
        lambda signal, kernel_taps: finish(signal, kernel_taps, segment), mixed, kernel
    )
    mixed_grad, kernel_part = pullback(cotangent.astype(jnp.float32))
    columns = context
    weight_share = lax.psum_scatter(
        jnp.einsum("rc,rd->cd", columns, mixed_grad, preferred_element_type=jnp.float32).astype(
            jnp.bfloat16
        ),
        "fsdp",
        scatter_dimension=0,
        tiled=True,
    ).astype(jnp.float32)
    context_grad = jnp.einsum(
        "rd,cd->rc",
        mixed_grad,
        lax.all_gather(out_weight, "fsdp", axis=0, tiled=True),
        preferred_element_type=jnp.float32,
    ).astype(jnp.bfloat16)
    frame_grad = attend_back(frames, soft_probs, rounded, context_grad)
    slot_total = incoming.shape[0]
    back_index = jnp.where(filled, compute_src, slot_total)
    returning = jnp.zeros_like(incoming).at[back_index].set(frame_grad, mode="drop")
    arrived = lax.all_to_all(returning, "dp", split_axis=0, concat_axis=0, tiled=True)
    source_index = jnp.where(present, send_rows, row_count)
    projected_grad = jnp.zeros_like(projected).at[source_index].set(arrived, mode="drop")
    scale_factor = (row_count * lax.axis_size("dp") * lax.axis_size("fsdp")) ** (-0.5)
    kernel_f = lax.psum(kernel_part, "fsdp")
    both = dp_allreduce_a2a(
        jnp.concatenate([weight_share, kernel_f, jnp.zeros((17, 1536), jnp.float32)], axis=0)
    )
    weight_total, kernel_total = (both[:48], both[48:79])
    return (
        result.astype(jnp.bfloat16),
        projected_grad,
        weight_total * scale_factor,
        kernel_total * scale_factor,
    )


def dp_allreduce_rs_ag(x):
    n = lax.axis_size("dp")
    flat = x.reshape(n, -1)
    part = lax.psum_scatter(flat, "dp", scatter_dimension=0, tiled=True)
    return lax.all_gather(part, "dp", axis=0, tiled=True).reshape(x.shape)


def dp_allreduce_a2a(x):
    n = lax.axis_size("dp")
    flat = x.reshape(n, -1)
    got = lax.all_to_all(flat, "dp", split_axis=0, concat_axis=0, tiled=True)
    part = jnp.sum(got, axis=0, keepdims=True)
    return lax.all_gather(part, "dp", axis=0, tiled=True).reshape(x.shape)


def dp_allreduce_a2a2(x):
    n = lax.axis_size("dp")
    flat = x.reshape(n, -1)
    got = lax.all_to_all(flat, "dp", split_axis=0, concat_axis=0, tiled=True)
    part = jnp.sum(got, axis=0, keepdims=True)
    back = lax.all_to_all(
        jnp.broadcast_to(part, flat.shape), "dp", split_axis=0, concat_axis=0, tiled=True
    )
    return back.reshape(x.shape)


def solution(mesh):
    placed = (
        P(("dp", "fsdp"), None),
        P("fsdp", None),
        P(),
        P(("dp", "fsdp"), None),
        P(("dp", "fsdp")),
        P(("dp", "fsdp")),
        P(("dp", "fsdp")),
    )
    return jax.shard_map(
        body,
        mesh=mesh,
        in_specs=placed,
        out_specs=(P(("dp", "fsdp"), None), P(("dp", "fsdp"), None), P("fsdp", None), P()),
        check_vma=False,
    )
```

profile of v0, /device:TPU:24, one launch (start us, length us, event | category | flops | bytes accessed | tf_op | source)
XLA Modules:
  0.0 341.6 jit_solution(10079741374050329405)
XLA Ops:
  7.9 1.2 compare_select_fusion.1
  9.1 1.0 gather_fusion
  10.3 1.0 all_to_all.22
  11.3 13.2 %all-to-all-start = ((bf16[32,4,2304]{2,1,0:T(4,128)(2,1)}), bf16[32,4,2304]{2,1,0:T(4,128)(2,1)S(1)}, u32[]{:S(2)}, u32[]{:S(2)}) async-start(bf16[32,4,2304]{2,1,0:T(4,128)(2,1)} %all_to_all.22), calls=%async_computation | async-start | bytes 1179648 | tf_op jit(solution)/shard_map/all_to_all | solution.py:84
  26.0 17.5 %all-to-all-done = bf16[32,4,2304]{2,1,0:T(4,128)(2,1)S(1)} async-done(((bf16[32,4,2304]{2,1,0:T(4,128)(2,1)}), bf16[32,4,2304]{2,1,0:T(4,128)(2,1)S(1)}, u32[]{:S(2)}, u32[]{:S(2)}) %all-to-all-start) | async-done | bytes 589856 | tf_op jit(solution)/shard_map/all_to_all | solution.py:84
  43.6 1.0 gather_fusion.1
  45.3 1.2 fusion.40
  47.0 9.4 %all-gather.4.cloned.1.call-done = bf16[768,1536]{1,0:T(8,128)(2,1)} async-done(((bf16[48,1536]{1,0:T(8,128)(2,1)}), bf16[768,1536]{1,0:T(8,128)(2,1)}) %all-gather.4.cloned.1.call-update) | async-done | bytes 2359312 | tf_op jit(solution)/shard_map/all_gather | solution.py:92
  56.4 2.2 fusion.2
  58.6 7.6 %multiply_reduce_fusion.31 = (f32[1536]{0:T(1024)}, f32[1536]{0:T(1024)}, f32[1536]{0:T(1024)}, f32[1536]{0:T(1024)}, f32[1536]{0:T(1024)}, /*index=5*/f32[1536]...) fusion(f32[128,1536]{1,0:T(8,128)S(1)} %fusion.2, ...), kind=kLoop, calls=%fused_computation.99 | loop fusion | flops 25152000 | bytes 3013632 | tf_op jit(solution)/shard_map/transpose(jvp())/reduce_sum | solution.py:74
  66.2 2.3 multiply_reduce_fusion.16
  70.5 2.6 multiply_reduce_fusion.4
  73.1 2.8 pad_add_fusion
  76.7 2.1 convolution_convert_fusion
  84.2 2.5 convolution_convert_fusion.5
  87.0 1.3 convolution_convert_fusion.2
  88.7 1.7 convolution_convert_fusion.3
  90.6 2.3 convolution_convert_fusion.4
  92.8 1.1 copy.42
  93.9 1.8 scatter_custom_fusion
  95.8 1.0 all_to_all.25
  96.8 10.3 %all-to-all-start.1 = ((bf16[32,4,2304]{2,1,0:T(4,128)(2,1)}), bf16[32,4,2304]{2,1,0:T(4,128)(2,1)S(1)}, u32[]{:S(2)}, u32[]{:S(2)}) async-start(bf16[32,4,2304]{2,1,0:T(4,128)(2,1)} %all_to_all.25), calls=%async_computation.1 | async-start | bytes 1179648 | tf_op jit(solution)/shard_map/all_to_all | solution.py:119
  107.2 2.4 multiply_reduce_fusion.22
  110.1 1.0 pad_add_fusion.7
  111.2 26.3 %reduce-scatter.2.cloned.1.call-done = bf16[48,1536]{1,0:T(8,128)(2,1)} async-done(((bf16[768,1536]{1,0:T(8,128)(2,1)}), bf16[48,1536]{1,0:T(8,128)(2,1)}) %reduce-scatter.2.cloned.1.call-update) | async-done | bytes 147472 | tf_op jit(solution)/shard_map/reduce_scatter | solution.py:101
  138.4 112.9 %all-reduce.66.cloned.1.call-done = f32[31,1536]{1,0:T(8,128)} async-done(((f32[31,1536]{1,0:T(8,128)}), f32[31,1536]{1,0:T(8,128)}) %all-reduce.66.cloned.1.call-update) | async-done | bytes 190480 | tf_op jit(solution)/shard_map/psum | solution.py:123
  251.3 1.0 maximum_maximum_fusion
  252.3 1.5 all_to_all.30
  253.8 10.2 %all-to-all-start.2 = ((f32[32,1,4608]{2,1,0:T(1,128)}), f32[32,1,4608]{2,1,0:T(1,128)S(1)}, u32[]{:S(2)}, u32[]{:S(2)}) async-start(f32[32,1,4608]{2,1,0:T(1,128)} %all_to_all.30), calls=%async_computation.3 | async-start | bytes 1179648 | tf_op jit(solution)/shard_map/all_to_all | solution.py:146
  264.2 2.4 scatter_custom_fusion.1
  266.6 17.0 %all-to-all-done.2 = f32[32,1,4608]{2,1,0:T(1,128)S(1)} async-done(((f32[32,1,4608]{2,1,0:T(1,128)}), f32[32,1,4608]{2,1,0:T(1,128)S(1)}, u32[]{:S(2)}, u32[]{:S(2)}) %all-to-all-start.2) | async-done | bytes 589856 | tf_op jit(solution)/shard_map/all_to_all | solution.py:146
  283.9 48.8 %all-gather.1 = f32[32,1,4608]{2,1,0:T(1,128)S(1)} all-gather(f32[1,1,4608]{2,1,0:T(1,128)S(1)} %reshape.348), channel_id=2, replica_groups=mesh['dp'=32,'fsdp'=16] {'dp'}, dimensions={0}, use_global_device_ids=true | all-gather | bytes 608256 | tf_op jit(solution)/shard_map/all_gather | solution.py:148
  (176 shorter events, 16.5 us)
Async XLA Ops:
  7.2 49.2 %all-gather.4.cloned.1.call-start = ((), (), s32[]{:S(2)}) async-start(), calls=%async_computation.4 | async-start | bytes 2506752 | tf_op jit(solution)/shard_map/all_gather | solution.py:92
  10.1 14.4 %copy-start.6 = (f32[31,1536]{1,0:T(8,128)S(1)}, f32[31,1536]{1,0:T(8,128)}, u32[]{:S(2)}) copy-start(f32[31,1536]{1,0:T(8,128)} %param.11) | copy-start | bytes 571396
  10.1 14.6 %copy-start.48 = (s32[128]{0:T(128)S(1)}, s32[128]{0:T(128)}, u32[]{:S(2)}) copy-start(s32[128]{0:T(128)} %param.14) | copy-start | bytes 1540
  10.1 15.5 %copy-start.46 = (s32[128]{0:T(128)S(1)}, s32[128]{0:T(128)}, u32[]{:S(2)}) copy-start(s32[128]{0:T(128)} %param.15) | copy-start | bytes 1540
  11.3 32.2 %all-to-all-start = ((bf16[32,4,2304]{2,1,0:T(4,128)(2,1)}), bf16[32,4,2304]{2,1,0:T(4,128)(2,1)S(1)}, u32[]{:S(2)}, u32[]{:S(2)}) async-start(bf16[32,4,2304]{2,1,0:T(4,128)(2,1)} %all_to_all.22), calls=%async_computation | async-start | bytes 1179648 | tf_op jit(solution)/shard_map/all_to_all | solution.py:84
  24.4 113.0 %reduce-scatter.2.cloned.1.call-start = ((), (), s32[]{:S(2)}) async-start(), calls=%async_computation.5 | async-start | bytes 2506752 | tf_op jit(solution)/shard_map/reduce_scatter | solution.py:101
  25.8 43.2 %copy-start.43 = (f32[128]{0:T(128)}, f32[128]{0:T(128)S(1)}, u32[]{:S(2)}) copy-start(f32[128]{0:T(128)S(1)} %get-tuple-element.120) | copy-start | bytes 1540
  25.8 43.2 %copy-start.44 = (f32[128]{0:T(128)}, f32[128]{0:T(128)S(1)}, u32[]{:S(2)}) copy-start(f32[128]{0:T(128)S(1)} %get-tuple-element.121) | copy-start | bytes 1540
  25.8 43.2 %copy-start.45 = (f32[128]{0:T(128)}, f32[128]{0:T(128)S(1)}, u32[]{:S(2)}) copy-start(f32[128]{0:T(128)S(1)} %get-tuple-element.122) | copy-start | bytes 1540
  25.8 43.9 %copy-start.37 = (f32[128]{0:T(128)}, f32[128]{0:T(128)S(1)}, u32[]{:S(2)}) copy-start(f32[128]{0:T(128)S(1)} %get-tuple-element.114) | copy-start | bytes 1540
  25.8 43.9 %copy-start.38 = (f32[128]{0:T(128)}, f32[128]{0:T(128)S(1)}, u32[]{:S(2)}) copy-start(f32[128]{0:T(128)S(1)} %get-tuple-element.115) | copy-start | bytes 1540
  25.8 43.9 %copy-start.39 = (f32[128]{0:T(128)}, f32[128]{0:T(128)S(1)}, u32[]{:S(2)}) copy-start(f32[128]{0:T(128)S(1)} %get-tuple-element.116) | copy-start | bytes 1540
  25.9 43.9 %copy-start.40 = (f32[128]{0:T(128)}, f32[128]{0:T(128)S(1)}, u32[]{:S(2)}) copy-start(f32[128]{0:T(128)S(1)} %get-tuple-element.117) | copy-start | bytes 1540
  25.9 43.9 %copy-start.41 = (f32[128]{0:T(128)}, f32[128]{0:T(128)S(1)}, u32[]{:S(2)}) copy-start(f32[128]{0:T(128)S(1)} %get-tuple-element.118) | copy-start | bytes 1540
  25.9 43.9 %copy-start.42 = (f32[128]{0:T(128)}, f32[128]{0:T(128)S(1)}, u32[]{:S(2)}) copy-start(f32[128]{0:T(128)S(1)} %get-tuple-element.119) | copy-start | bytes 1540
  26.0 20.5 %copy-start.36 = (pred[128,128]{0,1:T(8,128)(4,1)}, pred[128,128]{0,1:T(8,128)(4,1)S(1)}, u32[]{:S(2)}) copy-start(pred[128,128]{0,1:T(8,128)(4,1)S(1)} %broadcast_compare_fusion) | copy-start | bytes 49156
  44.9 42.0 %copy-start.2 = (bf16[128,768]{0,1:T(8,128)(2,1)}, bf16[128,768]{0,1:T(8,128)(2,1)S(1)}, u32[]{:S(2)}) copy-start(bf16[128,768]{0,1:T(8,128)(2,1)S(1)} %copy.36) | copy-start | bytes 589828
  95.7 14.1 %copy-start.10 = (f32[1536]{0:T(1024)S(1)}, f32[1536]{0:T(1024)}, u32[]{:S(2)}) copy-start(f32[1536]{0:T(1024)} %get-tuple-element.26) | copy-start | bytes 18436
  95.7 14.1 %copy-start.9 = (f32[1536]{0:T(1024)S(1)}, f32[1536]{0:T(1024)}, u32[]{:S(2)}) copy-start(f32[1536]{0:T(1024)} %get-tuple-element.27) | copy-start | bytes 18436
  95.7 14.1 %copy-start.8 = (f32[1536]{0:T(1024)S(1)}, f32[1536]{0:T(1024)}, u32[]{:S(2)}) copy-start(f32[1536]{0:T(1024)} %get-tuple-element.28) | copy-start | bytes 18436
  95.7 14.1 %copy-start.7 = (f32[1536]{0:T(1024)S(1)}, f32[1536]{0:T(1024)}, u32[]{:S(2)}) copy-start(f32[1536]{0:T(1024)} %get-tuple-element.29) | copy-start | bytes 18436
  95.7 14.1 %copy-start.17 = (f32[1536]{0:T(1024)S(1)}, f32[1536]{0:T(1024)}, u32[]{:S(2)}) copy-start(f32[1536]{0:T(1024)} %get-tuple-element.32) | copy-start | bytes 18436
  95.7 14.2 %copy-start.16 = (f32[1536]{0:T(1024)S(1)}, f32[1536]{0:T(1024)}, u32[]{:S(2)}) copy-start(f32[1536]{0:T(1024)} %get-tuple-element.33) | copy-start | bytes 18436
  95.8 14.2 %copy-start.15 = (f32[1536]{0:T(1024)S(1)}, f32[1536]{0:T(1024)}, u32[]{:S(2)}) copy-start(f32[1536]{0:T(1024)} %get-tuple-element.34) | copy-start | bytes 18436
  95.8 14.2 %copy-start.14 = (f32[1536]{0:T(1024)S(1)}, f32[1536]{0:T(1024)}, u32[]{:S(2)}) copy-start(f32[1536]{0:T(1024)} %get-tuple-element.35) | copy-start | bytes 18436
  95.8 14.2 %copy-start.27 = (f32[1,1536]{1,0:T(1,128)S(1)}, f32[1,1536]{1,0:T(1,128)}, u32[]{:S(2)}) copy-start(f32[1,1536]{1,0:T(1,128)} %reshape.271) | copy-start | bytes 18436
  95.8 14.2 %copy-start.28 = (f32[1,1536]{1,0:T(1,128)S(1)}, f32[1,1536]{1,0:T(1,128)}, u32[]{:S(2)}) copy-start(f32[1,1536]{1,0:T(1,128)} %reshape.272) | copy-start | bytes 18436
  95.8 14.2 %copy-start.29 = (f32[1,1536]{1,0:T(1,128)S(1)}, f32[1,1536]{1,0:T(1,128)}, u32[]{:S(2)}) copy-start(f32[1,1536]{1,0:T(1,128)} %reshape.273) | copy-start | bytes 18436
  95.8 14.2 %copy-start.30 = (f32[1,1536]{1,0:T(1,128)S(1)}, f32[1,1536]{1,0:T(1,128)}, u32[]{:S(2)}) copy-start(f32[1,1536]{1,0:T(1,128)} %reshape.274) | copy-start | bytes 18436
  96.8 157.1 %all-to-all-start.1 = ((bf16[32,4,2304]{2,1,0:T(4,128)(2,1)}), bf16[32,4,2304]{2,1,0:T(4,128)(2,1)S(1)}, u32[]{:S(2)}, u32[]{:S(2)}) async-start(bf16[32,4,2304]{2,1,0:T(4,128)(2,1)} %all_to_all.25), calls=%async_computation.1 | async-start | bytes 1179648 | tf_op jit(solution)/shard_map/all_to_all | solution.py:119
  107.1 144.2 %all-reduce.66.cloned.1.call-start = ((), (), s32[]{:S(2)}) async-start(), calls=%async_computation.6 | async-start | bytes 393216 | tf_op jit(solution)/shard_map/psum | solution.py:123
  253.8 29.7 %all-to-all-start.2 = ((f32[32,1,4608]{2,1,0:T(1,128)}), f32[32,1,4608]{2,1,0:T(1,128)S(1)}, u32[]{:S(2)}, u32[]{:S(2)}) async-start(f32[32,1,4608]{2,1,0:T(1,128)} %all_to_all.30), calls=%async_computation.3 | async-start | bytes 1179648 | tf_op jit(solution)/shard_map/all_to_all | solution.py:146
  (25 other events, 198.5 us)
Sparse Core Ops, SparseCore 0:
  10.1 46.2 all-gather.3
  78.9 58.4 reduce-scatter.1
  140.4 110.8 all-reduce.65
where the time goes:
time: 342 us
  waiting for transfers between devices  184 us (54%)
  blocking collectives  48.8 us (14%)
  starting transfers between devices  33.8 us (10%)
  other arithmetic  28.4 us (8%)
  local copies, waits for them, and re-layouts  17.9 us (5%)
  between operations  14.9 us (4%)
  matrix products  14 us (4%)
    psum x1, waiting for transfers between devices, body(): kernel_f = lax.psum(kernel_part, 'fsdp')  113 us
    all_gather x1, blocking collectives, dp_allreduce_a2a(): return lax.all_gather(part, 'dp', axis=0, tiled=True).reshape(x.shape)  48.8 us
    reduce_scatter x1, waiting for transfers between devices, body(): lax.psum_scatter(jnp.einsum('rc,rd->cd', columns, mixed_grad, preferred_e...  26.3 us
    all_to_all x1, waiting for transfers between devices, body(): lax.all_to_all(outgoing, 'dp', split_axis=0, concat_axis=0, tiled=True)  17.5 us
    all_to_all x1, waiting for transfers between devices, dp_allreduce_a2a(): got = lax.all_to_all(flat, 'dp', split_axis=0, concat_axis=0, tiled=True)  17 us
    reduce_sum x4, other arithmetic, finish(): kernel[offset] * padded[offset:offset + length] * matching[:, None]  14.9 us
    all_to_all x1, starting transfers between devices, body(): lax.all_to_all(outgoing, 'dp', split_axis=0, concat_axis=0, tiled=True)  13.2 us
    all_to_all x1, starting transfers between devices, body(): lax.all_to_all(returning, 'dp', split_axis=0, concat_axis=0, tiled=True)  10.3 us
  transfers between devices with their start and end apart: 6, of which 5 were waited for; matrix products, arithmetic and copies ran while one was open for 9% of the time, Pallas kernels for 0%

commit v1 on v0

--- a/solution.py
+++ b/solution.py
@@ -120,7 +120,7 @@
     source_index = jnp.where(present, send_rows, row_count)
     projected_grad = jnp.zeros_like(projected).at[source_index].set(arrived, mode="drop")
     scale_factor = (row_count * lax.axis_size("dp") * lax.axis_size("fsdp")) ** (-0.5)
-    kernel_f = lax.psum(kernel_part, "fsdp")
+    kernel_f = jnp.sum(lax.all_gather(kernel_part, "fsdp"), axis=0)
     both = dp_allreduce_a2a(
         jnp.concatenate([weight_share, kernel_f, jnp.zeros((17, 1536), jnp.float32)], axis=0)
     )

time: 342 us -> 278 us (0.81)
  the two profiles are of different devices: /device:TPU:24 before, /device:TPU:8 now
where the time goes in v1:
time: 278 us; the launch traced here: 277 us
  waiting for transfers between devices  125 us (45%)
  blocking collectives  48.6 us (17%)
  starting transfers between devices  33.7 us (12%)
  other arithmetic  29.2 us (11%)
  between operations  15 us (5%)
  matrix products  13.2 us (5%)
  local copies, waits for them, and re-layouts  12.2 us (4%)
    all_gather x1, blocking collectives, dp_allreduce_a2a(): return lax.all_gather(part, 'dp', axis=0, tiled=True).reshape(x.shape)  48.6 us
    all_gather x1, waiting for transfers between devices, body(): kernel_f = jnp.sum(lax.all_gather(kernel_part, 'fsdp'), axis=0)  47.1 us
    reduce_scatter x1, waiting for transfers between devices, body(): lax.psum_scatter(jnp.einsum('rc,rd->cd', columns, mixed_grad, preferred_e...  34.1 us
    all_to_all x1, waiting for transfers between devices, body(): lax.all_to_all(outgoing, 'dp', split_axis=0, concat_axis=0, tiled=True)  17.4 us
    all_to_all x1, waiting for transfers between devices, dp_allreduce_a2a(): got = lax.all_to_all(flat, 'dp', split_axis=0, concat_axis=0, tiled=True)  16.8 us
    reduce_sum x4, other arithmetic, finish(): kernel[offset] * padded[offset:offset + length] * matching[:, None]  14.6 us
    all_to_all x1, starting transfers between devices, body(): lax.all_to_all(outgoing, 'dp', split_axis=0, concat_axis=0, tiled=True)  13.2 us
    all_to_all x1, starting transfers between devices, body(): lax.all_to_all(returning, 'dp', split_axis=0, concat_axis=0, tiled=True)  10.2 us
  transfers between devices with their start and end apart: 6, of which 5 were waited for; matrix products, arithmetic and copies ran while one was open for 9% of the time, Pallas kernels for 0%

profile of v1, /device:TPU:8, one launch (start us, length us, event | category | flops | bytes accessed | tf_op | source)
XLA Modules:
  0.0 277.1 jit_solution(15437864007302919887)
XLA Ops:
  7.9 1.2 compare_select_fusion.1
  9.2 1.0 gather_fusion
  10.4 1.0 all_to_all.22
  11.3 13.2 %all-to-all-start = ((bf16[32,4,2304]{2,1,0:T(4,128)(2,1)}), bf16[32,4,2304]{2,1,0:T(4,128)(2,1)S(1)}, u32[]{:S(2)}, u32[]{:S(2)}) async-start(bf16[32,4,2304]{2,1,0:T(4,128)(2,1)} %all_to_all.22), calls=%async_computation | async-start | bytes 1179648 | tf_op jit(solution)/shard_map/all_to_all | solution.py:84
  26.1 17.4 %all-to-all-done = bf16[32,4,2304]{2,1,0:T(4,128)(2,1)S(1)} async-done(((bf16[32,4,2304]{2,1,0:T(4,128)(2,1)}), bf16[32,4,2304]{2,1,0:T(4,128)(2,1)S(1)}, u32[]{:S(2)}, u32[]{:S(2)}) %all-to-all-start) | async-done | bytes 589856 | tf_op jit(solution)/shard_map/all_to_all | solution.py:84
  43.6 1.0 gather_fusion.1
  45.3 1.2 fusion.40
  47.6 9.0 %all-gather.7.cloned.1.call-done = bf16[768,1536]{1,0:T(8,128)(2,1)} async-done(((bf16[48,1536]{1,0:T(8,128)(2,1)}), bf16[768,1536]{1,0:T(8,128)(2,1)}) %all-gather.7.cloned.1.call-update) | async-done | bytes 2359312 | tf_op jit(solution)/shard_map/all_gather | solution.py:92
  56.6 2.2 fusion.2
  58.8 7.8 %multiply_reduce_fusion.31 = (f32[1536]{0:T(1024)}, f32[1536]{0:T(1024)}, f32[1536]{0:T(1024)}, f32[1536]{0:T(1024)}, f32[1536]{0:T(1024)}, /*index=5*/f32[1536]...) fusion(f32[128,1536]{1,0:T(8,128)S(1)} %fusion.2, ...), kind=kLoop, calls=%fused_computation.99 | loop fusion | flops 25152000 | bytes 3013632 | tf_op jit(solution)/shard_map/transpose(jvp())/reduce_sum | solution.py:74
  66.6 2.2 multiply_reduce_fusion.16
  70.8 2.6 multiply_reduce_fusion.4
  73.5 2.6 pad_add_fusion
  76.9 2.2 convolution_convert_fusion
  79.6 2.0 multiply_reduce_fusion.22
  82.0 1.0 add_bitcast_fusion
  83.0 2.5 convolution_convert_fusion.5
  85.7 1.3 convolution_convert_fusion.2
  87.4 1.6 convolution_convert_fusion.3
  89.2 1.6 convolution_convert_fusion.4
  90.9 1.8 scatter_custom_fusion
  92.7 1.0 all_to_all.25
  93.6 10.2 %all-to-all-start.1 = ((bf16[32,4,2304]{2,1,0:T(4,128)(2,1)}), bf16[32,4,2304]{2,1,0:T(4,128)(2,1)S(1)}, u32[]{:S(2)}, u32[]{:S(2)}) async-start(bf16[32,4,2304]{2,1,0:T(4,128)(2,1)} %all_to_all.25), calls=%async_computation.1 | async-start | bytes 1179648 | tf_op jit(solution)/shard_map/all_to_all | solution.py:119
  103.9 34.1 %reduce-scatter.2.cloned.1.call-done = bf16[48,1536]{1,0:T(8,128)(2,1)} async-done(((bf16[768,1536]{1,0:T(8,128)(2,1)}), bf16[48,1536]{1,0:T(8,128)(2,1)}) %reduce-scatter.2.cloned.1.call-update) | async-done | bytes 147472 | tf_op jit(solution)/shard_map/reduce_scatter | solution.py:101
  138.0 0.9 convert_element_type.212
  138.9 47.1 %all-gather.9.cloned.1.call-done = f32[16,31,1536]{2,1,0:T(8,128)} async-done(((f32[1,31,1536]{2,1,0:T(8,128)}), f32[16,31,1536]{2,1,0:T(8,128)}) %all-gather.9.cloned.1.call-update) | async-done | bytes 3047440 | tf_op jit(solution)/shard_map/all_gather | solution.py:123
  186.1 2.1 reduce_sum.364
  188.3 1.5 all_to_all.30
  189.8 10.2 %all-to-all-start.2 = ((f32[32,1,4608]{2,1,0:T(1,128)}), f32[32,1,4608]{2,1,0:T(1,128)S(1)}, u32[]{:S(2)}, u32[]{:S(2)}) async-start(f32[32,1,4608]{2,1,0:T(1,128)} %all_to_all.30), calls=%async_computation.3 | async-start | bytes 1179648 | tf_op jit(solution)/shard_map/all_to_all | solution.py:146
  200.1 2.4 scatter_custom_fusion.1
  202.5 16.8 %all-to-all-done.2 = f32[32,1,4608]{2,1,0:T(1,128)S(1)} async-done(((f32[32,1,4608]{2,1,0:T(1,128)}), f32[32,1,4608]{2,1,0:T(1,128)S(1)}, u32[]{:S(2)}, u32[]{:S(2)}) %all-to-all-start.2) | async-done | bytes 589856 | tf_op jit(solution)/shard_map/all_to_all | solution.py:146
  219.7 48.6 %all-gather.3 = f32[32,1,4608]{2,1,0:T(1,128)S(1)} all-gather(f32[1,1,4608]{2,1,0:T(1,128)S(1)} %reshape.351), channel_id=3, replica_groups=mesh['dp'=32,'fsdp'=16] {'dp'}, dimensions={0}, use_global_device_ids=true | all-gather | bytes 608256 | tf_op jit(solution)/shard_map/all_gather | solution.py:148
  (173 shorter events, 11.1 us)
Async XLA Ops:
  7.2 49.4 %all-gather.7.cloned.1.call-start = ((), (), s32[]{:S(2)}) async-start(), calls=%async_computation.4 | async-start | bytes 2506752 | tf_op jit(solution)/shard_map/all_gather | solution.py:92
  10.2 14.4 %copy-start.4 = (f32[31,1536]{1,0:T(8,128)S(1)}, f32[31,1536]{1,0:T(8,128)}, u32[]{:S(2)}) copy-start(f32[31,1536]{1,0:T(8,128)} %param.11) | copy-start | bytes 571396
  10.2 14.6 %copy-start.46 = (s32[128]{0:T(128)S(1)}, s32[128]{0:T(128)}, u32[]{:S(2)}) copy-start(s32[128]{0:T(128)} %param.14) | copy-start | bytes 1540
  10.2 15.5 %copy-start.44 = (s32[128]{0:T(128)S(1)}, s32[128]{0:T(128)}, u32[]{:S(2)}) copy-start(s32[128]{0:T(128)} %param.15) | copy-start | bytes 1540
  11.3 32.2 %all-to-all-start = ((bf16[32,4,2304]{2,1,0:T(4,128)(2,1)}), bf16[32,4,2304]{2,1,0:T(4,128)(2,1)S(1)}, u32[]{:S(2)}, u32[]{:S(2)}) async-start(bf16[32,4,2304]{2,1,0:T(4,128)(2,1)} %all_to_all.22), calls=%async_computation | async-start | bytes 1179648 | tf_op jit(solution)/shard_map/all_to_all | solution.py:84
  24.5 113.5 %reduce-scatter.2.cloned.1.call-start = ((), (), s32[]{:S(2)}) async-start(), calls=%async_computation.5 | async-start | bytes 2506752 | tf_op jit(solution)/shard_map/reduce_scatter | solution.py:101
  25.9 43.4 %copy-start.38 = (f32[128]{0:T(128)}, f32[128]{0:T(128)S(1)}, u32[]{:S(2)}) copy-start(f32[128]{0:T(128)S(1)} %get-tuple-element.120) | copy-start | bytes 1540
  25.9 43.4 %copy-start.40 = (f32[128]{0:T(128)}, f32[128]{0:T(128)S(1)}, u32[]{:S(2)}) copy-start(f32[128]{0:T(128)S(1)} %get-tuple-element.121) | copy-start | bytes 1540
  25.9 43.4 %copy-start.42 = (f32[128]{0:T(128)}, f32[128]{0:T(128)S(1)}, u32[]{:S(2)}) copy-start(f32[128]{0:T(128)S(1)} %get-tuple-element.122) | copy-start | bytes 1540
  25.9 44.2 %copy-start.26 = (f32[128]{0:T(128)}, f32[128]{0:T(128)S(1)}, u32[]{:S(2)}) copy-start(f32[128]{0:T(128)S(1)} %get-tuple-element.114) | copy-start | bytes 1540
  25.9 44.2 %copy-start.28 = (f32[128]{0:T(128)}, f32[128]{0:T(128)S(1)}, u32[]{:S(2)}) copy-start(f32[128]{0:T(128)S(1)} %get-tuple-element.115) | copy-start | bytes 1540
  25.9 44.2 %copy-start.30 = (f32[128]{0:T(128)}, f32[128]{0:T(128)S(1)}, u32[]{:S(2)}) copy-start(f32[128]{0:T(128)S(1)} %get-tuple-element.116) | copy-start | bytes 1540
  25.9 44.2 %copy-start.32 = (f32[128]{0:T(128)}, f32[128]{0:T(128)S(1)}, u32[]{:S(2)}) copy-start(f32[128]{0:T(128)S(1)} %get-tuple-element.117) | copy-start | bytes 1540
  25.9 44.2 %copy-start.34 = (f32[128]{0:T(128)}, f32[128]{0:T(128)S(1)}, u32[]{:S(2)}) copy-start(f32[128]{0:T(128)S(1)} %get-tuple-element.118) | copy-start | bytes 1540
  26.0 44.2 %copy-start.36 = (f32[128]{0:T(128)}, f32[128]{0:T(128)S(1)}, u32[]{:S(2)}) copy-start(f32[128]{0:T(128)S(1)} %get-tuple-element.119) | copy-start | bytes 1540
  26.1 20.4 %copy-start.25 = (pred[128,128]{0,1:T(8,128)(4,1)}, pred[128,128]{0,1:T(8,128)(4,1)S(1)}, u32[]{:S(2)}) copy-start(pred[128,128]{0,1:T(8,128)(4,1)S(1)} %broadcast_compare_fusion) | copy-start | bytes 49156
  45.1 11.5 %copy-start.2 = (bf16[128,768]{0,1:T(8,128)(2,1)}, bf16[128,768]{0,1:T(8,128)(2,1)S(1)}, u32[]{:S(2)}) copy-start(bf16[128,768]{0,1:T(8,128)(2,1)S(1)} %copy.35) | copy-start | bytes 589828
  47.6 11.2 %copy-start.1 = (bf16[128,1536]{1,0:T(8,128)(2,1)S(1)}, bf16[128,1536]{1,0:T(8,128)(2,1)}, u32[]{:S(2)}) copy-start(bf16[128,1536]{1,0:T(8,128)(2,1)} %param.12) | copy-start | bytes 1179652
  76.8 2.6 copy-start.27
  79.1 2.6 copy-start.8
  79.1 2.7 copy-start.7
  79.1 2.7 copy-start.6
  79.1 2.7 copy-start.5
  79.1 2.7 copy-start.24
  79.2 2.8 copy-start.23
  79.2 2.8 copy-start.22
  79.2 2.8 %copy-start.21 = (f32[1536]{0:T(1024)S(1)}, f32[1536]{0:T(1024)}, u32[]{:S(2)}) copy-start(f32[1536]{0:T(1024)} %get-tuple-element.35) | copy-start | bytes 18436
  79.2 106.9 %all-gather.9.cloned.1.call-start = ((), (), s32[]{:S(2)}) async-start(), calls=%async_computation.6 | async-start | bytes 3342336 | tf_op jit(solution)/shard_map/all_gather | solution.py:123
  81.5 4.2 %copy-start.3 = (bf16[128,768]{0,1:T(8,128)(2,1)S(1)}, bf16[128,768]{0,1:T(8,128)(2,1)}, u32[]{:S(2)}) copy-start(bf16[128,768]{0,1:T(8,128)(2,1)} %copy-done.2) | copy-start | bytes 589828
  81.5 4.2 %copy-start.48 = (f32[8,128]{1,0:T(8,128)S(1)}, f32[8,128]{1,0:T(8,128)}, u32[]{:S(2)}) copy-start(f32[8,128]{1,0:T(8,128)} %copy-done.47) | copy-start | bytes 12292
  93.6 96.2 %all-to-all-start.1 = ((bf16[32,4,2304]{2,1,0:T(4,128)(2,1)}), bf16[32,4,2304]{2,1,0:T(4,128)(2,1)S(1)}, u32[]{:S(2)}, u32[]{:S(2)}) async-start(bf16[32,4,2304]{2,1,0:T(4,128)(2,1)} %all_to_all.25), calls=%async_computation.1 | async-start | bytes 1179648 | tf_op jit(solution)/shard_map/all_to_all | solution.py:119
  189.8 29.6 %all-to-all-start.2 = ((f32[32,1,4608]{2,1,0:T(1,128)}), f32[32,1,4608]{2,1,0:T(1,128)S(1)}, u32[]{:S(2)}, u32[]{:S(2)}) async-start(f32[32,1,4608]{2,1,0:T(1,128)} %all_to_all.30), calls=%async_computation.3 | async-start | bytes 1179648 | tf_op jit(solution)/shard_map/all_to_all | solution.py:146
  (23 other events, 55.6 us)
Sparse Core Ops, SparseCore 0:
  10.1 46.4 all-gather.6
  79.3 58.6 reduce-scatter.1
  140.7 45.3 all-gather.8
